TPU v7x, 32 devices: a whole 2x2x4 slice. The times are simulated.
32 devices in a mesh: dp: 4 (over y, x), expert: 8 (over z, core).
Axes of the slice: x: 2, y: 2, z: 4, core: 2. Of those that a mesh axis runs over, the one named last changes fastest.
Arguments:
- hidden: bfloat16 [32, 2048], P(('dp', 'expert')), may hold values from -6 to 6
- attn_gain: float32 [2048], replicated, may hold values from 0.25 to 1.75
- query_weight: bfloat16 [3072, 2048], P('expert'), may hold values from -0.125 to 0.125
- latent_down: bfloat16 [2048, 576], replicated, may hold values from -0.125 to 0.125
- latent_up: bfloat16 [512, 4096], P(None, 'expert'), may hold values from -0.25 to 0.25
- out_weight: bfloat16 [2048, 2048], P('expert'), may hold values from -0.125 to 0.125
- latent_pool: bfloat16 [128, 32, 576], P('dp'), may hold values from -1000 to 1000
- page_table: int32 [32, 16], replicated, may hold values from -1 to 127, as said below
- page_counts: int32 [32], replicated, may hold values from 1 to 16, as said below
- ffn_gain: float32 [2048], replicated, may hold values from 0.25 to 1.75
- expert_ids: int32 [32, 6], replicated, may hold values from 0 to 23, all different within a row; in each aligned block of 32 rows (0 to 31, 32 to 63, ...) at most 16 rows name the same one
- expert_gates: float32 [32, 6], replicated, may hold values from 0.05 to 0.6
- old_place: int32 [8, 4], replicated, may hold values from 0 to 23, as said below
- new_place: int32 [8, 4], replicated, may hold values from 0 to 23, as said below
- expert_gate_up: bfloat16 [32, 2, 1408, 2048], P('expert', None, None, 'dp'), as said below
- expert_down: bfloat16 [32, 1408, 2048], P('expert', None, 'dp'), as said below
- shared_gate_up: bfloat16 [2, 2816, 2048], P(None, None, 'dp'), may hold values from -0.125 to 0.125
- shared_down: bfloat16 [2816, 2048], P(None, 'dp'), may hold values from -0.109375 to 0.109375
Outputs:
- layer_out: bfloat16 [32, 2048], P(('dp', 'expert'))
- moved_gate_up: bfloat16 [32, 2, 1408, 2048], P('expert', None, None, 'dp')
- moved_down: bfloat16 [32, 1408, 2048], P('expert', None, 'dp')
Inputs may be any that keep to these rules, and one draw needn't show every extreme that they name: `page_counts`: each request's count of cached pages; exactly one request has 16. `page_table`: row t names page_counts[t] pages of the pool, no page named twice in the table; its other entries are -1. Page p lies on dp index p // 32. `expert_ids`: no expert is named by more than 16 tokens in all; some expert by exactly 16. `old_place`: row i holds the experts of the slots on expert index i, slot s of row i being global slot i * 4 + s; every expert is held by one slot or more. `new_place`: equal to old_place except in exactly one slot of each row, which names another expert. `expert_gate_up`: slots that hold the same expert under old_place hold equal weights. `expert_down`: slots that hold the same expert under old_place hold equal weights.
All inputs are finite; a program needn't handle non-finite values.
Results may differ from a plain program's by a relative error of at most 0.02.
Values may be sent and summed in bfloat16 or wider, within the bound.
No kernel may reach another device: no remote copies, remote signals or barrier semaphores. Data moves between devices by JAX's collectives and lax.ppermute only.
A program may use at most 128 MiB of HBM per device.

v0:
```python
import math
import jax
import jax.numpy as jnp
from jax import lax
from jax.sharding import PartitionSpec as P

NOPE = 128
ROPE = 64
VHEAD = 128
LATENT = 512
EXP_DEV = 3
PAGE = 32
EPSILON = 1e-06
ROPE_BASE = 50000.0
MASKED_SCORE = -1e30
HIGHEST = lax.Precision.HIGHEST


def rms_plain(values):
    mean_square = jnp.mean(values * values, axis=-1, keepdims=True)
    return values * lax.rsqrt(mean_square + EPSILON)


def rms_norm(values, norm_gain):
    return rms_plain(values) * norm_gain


def rotary(values, position):
    half_width = values.shape[-1] // 2
    exponent = jnp.arange(half_width).astype(jnp.float32) * (2.0 / values.shape[-1])
    frequency = jnp.exp(-exponent * math.log(ROPE_BASE))
    angles = position[..., None] * frequency
    cosine = jnp.cos(angles)
    sine_part = jnp.sin(angles)
    first_half = values[..., :half_width]
    second = values[..., half_width:]
    return jnp.concatenate(
        [first_half * cosine - second * sine_part, second * cosine + first_half * sine_part],
        axis=-1,
    )


def gather_rows(rows):
    by_expert = lax.all_gather(rows, "expert", axis=0, tiled=True)
    return lax.all_gather(by_expert, "dp", axis=0, tiled=True)


def spread_slots(gate_up, down, picks, ex_count):
    chosen = jnp.concatenate([gate_up[picks], down[picks][:, None]], axis=1)
    count, parts, ff_width, col_width = chosen.shape
    pieces = chosen.reshape(count, parts, ex_count, ff_width // ex_count, col_width)
    spread = lax.all_to_all(pieces, "expert", split_axis=2, concat_axis=0, tiled=True)
    return spread.reshape(ex_count * count, parts, ff_width // ex_count, col_width)


def migrate(expert_gate_up, expert_down, old_place, new_place, ex_index):
    rows, slots_local = old_place.shape
    slots = rows * slots_local
    ex_count = rows
    ff_width = expert_gate_up.shape[2]
    changed = old_place != new_place
    moved_slot = jnp.argmax(changed, axis=1)
    wanted = jnp.take_along_axis(new_place, moved_slot[:, None], axis=1)[:, 0]
    hit = old_place.reshape(-1)[None, :] == wanted[:, None]
    first = jnp.argmax(hit, axis=1).astype(jnp.int32)
    last = (slots - 1 - jnp.argmax(hit[:, ::-1], axis=1)).astype(jnp.int32)
    slot_ids = jnp.arange(slots, dtype=jnp.int32)

    def needed_of(src):
        needed = jnp.any(src[:, None] == slot_ids[None, :], axis=0).reshape(rows, slots_local)
        return (needed, jnp.max(jnp.sum(needed.astype(jnp.int32), axis=1)))

    need_first, load_first = needed_of(first)
    need_last, load_last = needed_of(last)
    use_last = load_last < load_first
    source = jnp.where(use_last, last, first)
    needed = jnp.where(use_last, need_last, need_first)
    load = jnp.minimum(load_first, load_last)
    rank = jnp.cumsum(needed.astype(jnp.int32), axis=1) - 1
    local_ids = jnp.arange(slots_local, dtype=jnp.int32)
    picks = jnp.stack(
        [jnp.argmax(needed & (rank == k), axis=1).astype(jnp.int32) for k in range(slots_local)],
        axis=1,
    )
    my_picks = picks[ex_index]
    src_dev = source // slots_local
    src_rank = rank.reshape(-1)[source]
    fast = min(2, slots_local)
    spread_a = spread_slots(expert_gate_up, expert_down, my_picks[:fast], ex_count)
    out_a = spread_a[src_dev * fast + jnp.minimum(src_rank, fast - 1)]
    if slots_local > fast:
        rest = slots_local - fast

        def extra():
            spread_b = spread_slots(expert_gate_up, expert_down, my_picks[fast:], ex_count)
            return spread_b[src_dev * rest + jnp.clip(src_rank - fast, 0, rest - 1)]

        out_b = lax.cond(load > fast, extra, lambda: jnp.zeros_like(out_a))
        out_a = jnp.where((src_rank < fast)[:, None, None, None], out_a, out_b)
    arrived = lax.all_to_all(out_a, "expert", split_axis=0, concat_axis=2, tiled=True)
    is_moved = local_ids == moved_slot[ex_index]
    moved_gate_up = jnp.where(is_moved[:, None, None, None], arrived[:, :2], expert_gate_up)
    moved_down = jnp.where(is_moved[:, None, None], arrived[:, 2], expert_down)
    return (moved_gate_up, moved_down)


def local(
    hidden,
    attn_gain,
    query_weight,
    latent_down,
    latent_up,
    out_weight,
    latent_pool,
    page_table,
    page_counts,
    ffn_gain,
    expert_ids,
    expert_gates,
    old_place,
    new_place,
    expert_gate_up,
    expert_down,
    shared_gate_up,
    shared_down,
):
    dp_count = lax.axis_size("dp")
    ex_count = lax.axis_size("expert")
    dp_index = lax.axis_index("dp")
    ex_index = lax.axis_index("expert")
    req_local = hidden.shape[0]
    group_rows = req_local * ex_count
    requests = page_counts.shape[0]
    head_local = query_weight.shape[0] // (NOPE + ROPE)
    score_scale = (NOPE + ROPE) ** (-0.5)
    group_start = dp_index * group_rows
    everyone = gather_rows(hidden)
    normed = rms_norm(everyone.astype(jnp.float32), attn_gain).astype(jnp.bfloat16)
    queries = jnp.einsum(
        "td,qd->tq", normed, query_weight, preferred_element_type=jnp.float32
    ).reshape(requests, head_local, NOPE + ROPE)
    position = (page_counts * PAGE).astype(jnp.float32)
    query_rope = rotary(queries[..., NOPE:], position[:, None]).astype(jnp.bfloat16)
    up_table = latent_up.reshape(LATENT, head_local, NOPE + VHEAD)
    query_latent = jnp.einsum(
        "thn,lhn->thl",
        queries[..., :NOPE],
        up_table[..., :NOPE].astype(jnp.float32),
        precision=HIGHEST,
    ).astype(jnp.bfloat16)
    pages_local = latent_pool.shape[0]
    pool_total = pages_local * dp_count
    flat_pages = page_table.reshape(-1)
    flat_owner = jnp.repeat(jnp.arange(requests, dtype=jnp.int32), page_table.shape[1])
    target = jnp.where(flat_pages >= 0, flat_pages, pool_total)
    owner_all = jnp.full((pool_total,), -1, jnp.int32).at[target].set(flat_owner, mode="drop")
    page_owner = lax.dynamic_slice_in_dim(owner_all, dp_index * pages_local, pages_local)
    page_used = page_owner >= 0
    owner_safe = jnp.maximum(page_owner, 0)
    page_latent = latent_pool[..., :LATENT]
    page_rope = latent_pool[..., LATENT:]
    scores = jnp.einsum(
        "phl,pkl->phk", query_latent[owner_safe], page_latent, preferred_element_type=jnp.float32
    )
    scores = (
        scores
        + jnp.einsum(
            "phr,pkr->phk", query_rope[owner_safe], page_rope, preferred_element_type=jnp.float32
        )
    ) * score_scale
    raw_max = jnp.max(scores, axis=2)
    weights = jnp.exp(scores - raw_max[..., None])
    page_total = jnp.sum(weights, axis=2)
    page_mix = jnp.einsum(
        "phk,pkl->phl",
        weights.astype(jnp.bfloat16),
        page_latent,
        preferred_element_type=jnp.float32,
    )
    page_max = jnp.where(page_used[:, None], raw_max, MASKED_SCORE)
    member = page_owner[None, :] == jnp.arange(requests, dtype=jnp.int32)[:, None]
    req_max = jnp.max(jnp.where(member[:, :, None], page_max[None], MASKED_SCORE), axis=1)
    rescale = jnp.where(page_used[:, None], jnp.exp(page_max - req_max[owner_safe]), 0.0)
    member_float = member.astype(jnp.float32)
    req_total = jnp.dot(member_float, page_total * rescale, precision=HIGHEST)
    req_mix = jnp.einsum(
        "rp,phl->rhl", member_float, page_mix * rescale[..., None], precision=HIGHEST
    )
    packed = jnp.concatenate([req_mix, req_max[..., None], req_total[..., None]], axis=-1)
    gathered = lax.all_gather(packed, "dp", axis=0, tiled=False)
    gathered = lax.dynamic_slice_in_dim(gathered, group_start, group_rows, 1)
    each_max = gathered[..., LATENT]
    part_max = jnp.max(each_max, axis=0)
    each_weight = jnp.exp(each_max - part_max[None])
    part_total = jnp.sum(gathered[..., LATENT + 1] * each_weight, axis=0)
    part_mix = jnp.sum(gathered[..., :LATENT] * each_weight[..., None], axis=0)
    own_normed = lax.dynamic_slice_in_dim(normed, group_start, group_rows, 0)
    own_position = lax.dynamic_slice_in_dim(position, group_start, group_rows, 0)
    fresh_latent = jnp.dot(own_normed, latent_down, preferred_element_type=jnp.float32)
    new_latent = rms_plain(fresh_latent[:, :LATENT]).astype(jnp.bfloat16)
    new_rope = rotary(fresh_latent[:, LATENT:], own_position).astype(jnp.bfloat16)
    own_query = lax.dynamic_slice_in_dim(query_latent, group_start, group_rows, 0)
    own_rope_query = lax.dynamic_slice_in_dim(query_rope, group_start, group_rows, 0)
    own_score = jnp.einsum("thl,tl->th", own_query, new_latent, preferred_element_type=jnp.float32)
    own_score = (
        own_score
        + jnp.einsum("thr,tr->th", own_rope_query, new_rope, preferred_element_type=jnp.float32)
    ) * score_scale
    highest = jnp.maximum(part_max, own_score)
    kept_part = jnp.exp(part_max - highest)
    own_weight = jnp.exp(own_score - highest)
    denominator = part_total * kept_part + own_weight
    numerator = (
        part_mix * kept_part[..., None]
        + own_weight[..., None] * new_latent.astype(jnp.float32)[:, None, :]
    )
    attended = (numerator / denominator[..., None]).astype(jnp.bfloat16)
    heads_out = jnp.einsum(
        "thl,lhv->thv", attended, up_table[..., NOPE:], preferred_element_type=jnp.float32
    )
    heads_out = heads_out.astype(jnp.bfloat16).reshape(group_rows, head_local * VHEAD)
    partial_value = jnp.dot(heads_out, out_weight, preferred_element_type=jnp.float32)
    attn_out = lax.psum_scatter(partial_value, "expert", scatter_dimension=0, tiled=True)
    residual = hidden.astype(jnp.float32) + attn_out
    normed_ffn = rms_norm(residual, ffn_gain).astype(jnp.bfloat16)
    slots_local = expert_gate_up.shape[0]
    ff_width = expert_gate_up.shape[2]
    col_width = expert_gate_up.shape[3]
    every_row = gather_rows(normed_ffn)
    my_columns = lax.dynamic_slice_in_dim(every_row, dp_index * col_width, col_width, 1)
    by_group = my_columns.reshape(dp_count, ex_count, req_local, col_width).transpose(1, 0, 2, 3)
    ffn_rows = by_group.reshape(requests, col_width)
    column_rows = lax.dynamic_index_in_dim(by_group, ex_index, 0, keepdims=False).reshape(
        dp_count * req_local, col_width
    )
    top_count = expert_ids.shape[1]
    experts_count = EXP_DEV * ex_count
    ids_order = (
        expert_ids.reshape(dp_count, ex_count, req_local, top_count)
        .transpose(1, 0, 2, 3)
        .reshape(requests, top_count)
    )
    gates_order = (
        expert_gates.reshape(dp_count, ex_count, req_local, top_count)
        .transpose(1, 0, 2, 3)
        .reshape(requests, top_count)
    )
    old_flat = old_place.reshape(-1)
    holds_map = old_flat[None, :] == jnp.arange(experts_count, dtype=jnp.int32)[:, None]
    holder = jnp.argmax(holds_map, axis=1)
    slot_of = holder[ids_order.reshape(-1)]
    capacity = 2 * requests * top_count // experts_count
    local_slot = slot_of - ex_index * slots_local
    slot_hot = local_slot[:, None] == jnp.arange(slots_local, dtype=jnp.int32)[None, :]
    slot_rank = jnp.cumsum(slot_hot.astype(jnp.int32), axis=0) - 1
    position_in = jnp.where(slot_hot, slot_rank, capacity)
    route_hot = (
        position_in[:, :, None] == jnp.arange(capacity, dtype=jnp.int32)[None, None, :]
    ).astype(jnp.float32)
    route_hot = route_hot.reshape(requests, top_count, slots_local, capacity)
    dispatch = jnp.sum(route_hot, axis=1).astype(jnp.bfloat16)
    combine = jnp.sum(route_hot * gates_order[:, :, None, None], axis=1)
    slot_inputs = jnp.einsum(
        "tsc,td->scd", dispatch, ffn_rows, preferred_element_type=jnp.float32
    ).astype(jnp.bfloat16)
    routed_part = jnp.einsum(
        "scd,sgfd->sgcf", slot_inputs, expert_gate_up, preferred_element_type=jnp.float32
    )
    shared_part = jnp.einsum(
        "td,gfd->gtf", column_rows, shared_gate_up, preferred_element_type=jnp.float32
    )
    routed_sum, shared_sum = lax.psum((routed_part, shared_part), "dp")
    activated = (jax.nn.silu(routed_sum[:, 0]) * routed_sum[:, 1]).astype(jnp.bfloat16)
    slot_out = jnp.einsum(
        "scf,sfd->scd", activated, expert_down, preferred_element_type=jnp.float32
    )
    routed = jnp.einsum("tsc,scd->td", combine, slot_out, precision=HIGHEST)
    shared_act = (jax.nn.silu(shared_sum[0]) * shared_sum[1]).astype(jnp.bfloat16)
    shared_term = jnp.dot(shared_act, shared_down, preferred_element_type=jnp.float32)
    moe_rows = lax.psum_scatter(routed, "expert", scatter_dimension=0, tiled=True)
    moe_part = lax.all_to_all(moe_rows + shared_term, "dp", split_axis=0, concat_axis=1, tiled=True)
    layer_out = (residual + moe_part).astype(jnp.bfloat16)
    moved_gate_up, moved_down = migrate(expert_gate_up, expert_down, old_place, new_place, ex_index)
    return (layer_out, moved_gate_up, moved_down)


def solution(mesh):
    in_specs = (
        P(("dp", "expert"), None),
        P(),
        P("expert", None),
        P(),
        P(None, "expert"),
        P("expert", None),
        P("dp", None, None),
        P(),
        P(),
        P(),
        P(),
        P(),
        P(),
        P(),
        P("expert", None, None, "dp"),
        P("expert", None, "dp"),
        P(None, None, "dp"),
        P(None, "dp"),
    )
    out_specs = (P(("dp", "expert"), None), P("expert", None, None, "dp"), P("expert", None, "dp"))
    return jax.shard_map(local, mesh=mesh, in_specs=in_specs, out_specs=out_specs, check_vma=False)
```

profile of v0, /device:TPU:0, one launch (start us, length us, event | category | flops | bytes accessed | tf_op | source)
XLA Modules:
  0.0 691.7 jit_solution(8807751896408755276)
XLA Ops:
  18.1 5.9 mini-gather-slice.2
  24.0 5.2 mini-gather-slice.3
  30.6 5.2 gather_fusion.11
  35.8 4.7 gather_fusion.12
  40.5 5.0 gather_fusion.8
  45.5 5.6 pad_maximum_fusion.3
  51.1 7.7 %pad_maximum_fusion.2 = bf16[2,3,8,176,512]{4,3,2,1,0:T(8,128)(2,1)} fusion(bf16[2,1,8,176,512]{4,3,2,1,0:T(8,128)(2,1)} %bitcast.229, bf16[2,2,8,176,512]{4,3,2,1,0:T(8,128)(2,1)} %bitcast.225), kind=kLoop, calls=%fused_computation.22 | loop fusion | flops 4325376 | bytes 17301504 | tf_op jit(solution)/shard_map/concatenate | solution.py:49
  58.8 7.6 %copy.166 = bf16[2,3,8,176,512]{4,3,1,0,2:T(8,128)(2,1)} copy(bf16[2,3,8,176,512]{4,3,2,1,0:T(8,128)(2,1)} %pad_maximum_fusion.2) | data formatting | bytes 17301504 | tf_op jit(solution)/shard_map/concatenate | solution.py:49
  68.7 2.5 conditional.1
  68.7 2.5 broadcast.321
  71.3 6.5 all-to-all-start.2
  77.8 195.6 %all-gather.1 = bf16[8,1,2048]{2,1,0:T(2,128)(2,1)S(1)} all-gather(bf16[1,1,2048]{2,1,0:T(2,128)(2,1)S(1)} %bitcast.240), channel_id=1, replica_groups=mesh['dp'=4,'expert'=8] {'expert'}, dimensions={0}, use_global_device_ids=true | all-gather | bytes 36864 | tf_op jit(solution)/shard_map/all_gather | solution.py:44
  273.4 8.5 %all_gather.19 = bf16[32,2048]{1,0:T(8,128)(2,1)S(1)} all-gather(bf16[8,2048]{1,0:T(8,128)(2,1)S(1)} %bitcast.236), channel_id=1, replica_groups=mesh['dp'=4,'expert'=8] {'dp'}, dimensions={0}, use_global_device_ids=true | all-gather | bytes 163840 | tf_op jit(solution)/shard_map/all_gather | solution.py:45
  282.2 2.0 fusion.91
  289.1 2.6 scatter_custom_fusion
  297.2 2.3 gather_fusion.4
  299.4 1.6 fusion.6
  301.0 1.9 fusion.90
  304.2 1.4 copy.148
  311.3 1.4 convolution_bitcast_fusion.3
  312.7 1.4 copy.152
  314.0 1.3 copy.151
  316.7 1.6 convolution_multiply_fusion
  320.0 11.4 %all-gather = f32[128,2,514]{2,0,1:T(8,128)S(1)} all-gather(f32[32,2,514]{2,0,1:T(8,128)S(1)} %pad_maximum_fusion.4), channel_id=2, replica_groups=mesh['dp'=4,'expert'=8] {'dp'}, dimensions={0}, use_global_device_ids=true | all-gather | bytes 657920 | tf_op jit(solution)/shard_map/all_gather | solution.py:190
  333.8 1.5 copy.183
  335.2 2.4 fusion.26
  343.7 1.7 copy.181
  345.4 3.0 multiply_reduce_fusion
  350.0 2.4 fusion.8
  354.8 4.5 compare_select_fusion.5
  359.4 10.5 %select_subtract_fusion = s32[192]{0:T(256)S(1)} fusion(pred[192]{0:T(512)(128)(4,1)S(1)} %get-tuple-element.86, pred[192]{0:T(512)(128)(4,1)S(1)} %get-tuple-element.85, pred[192]{0:T(512)(128)(4,1)S(1)} %get-tuple-element.84, pred[192]{0:T(512)(128)(4,1)S(1)} %get-tuple-element.83, pred[192]{0:T(512)(128)(4,1)S(1)} %get-tuple-element.82, ...), kind=kLoop, calls=%fused_computation.212 | loop fusion | flops 3456 | bytes 4872 | tf_op jit(solution)/shard_map/sub | solution.py:253
  372.7 32.9 %all-reduce.8.cloned.1.call-done = f32[8,2048]{1,0:T(8,128)} async-done(((f32[8,2048]{1,0:T(8,128)}), f32[8,2048]{1,0:T(8,128)}) %all-reduce.8.cloned.1.call-update) | async-done | bytes 65552
  405.6 2.1 multiply_reduce_fusion.2
  408.4 14.0 %all-gather.2 = bf16[8,1,2048]{2,1,0:T(2,128)(2,1)S(1)} all-gather(bf16[1,1,2048]{2,1,0:T(2,128)(2,1)S(1)} %convert_bitcast_fusion), channel_id=1, replica_groups=mesh['dp'=4,'expert'=8] {'expert'}, dimensions={0}, use_global_device_ids=true | all-gather | bytes 36864 | tf_op jit(solution)/shard_map/all_gather | solution.py:44
  422.4 8.4 %all_gather.23 = bf16[32,2048]{1,0:T(8,128)(2,1)S(1)} all-gather(bf16[8,2048]{1,0:T(8,128)(2,1)S(1)} %bitcast.237), channel_id=1, replica_groups=mesh['dp'=4,'expert'=8] {'dp'}, dimensions={0}, use_global_device_ids=true | all-gather | bytes 163840 | tf_op jit(solution)/shard_map/all_gather | solution.py:45
  430.9 4.9 convolution_bitcast_fusion
  435.8 6.9 convolution_bitcast_fusion.1
  443.4 46.9 %all-reduce.12.cloned.1.call-done = (f32[2,4,2816]{2,1,0:T(4,128)}, f32[4,2,16,1408]{3,2,1,0:T(8,128)}) async-done(((f32[2,4,2816]{2,1,0:T(4,128)}, f32[4,2,16,1408]{3,2,1,0:T(8,128)}), (f32[2,4,2816]{2,1,0:T(4,128)}, f32[4,2,16,1408]{3,2,1,0:T(8,128)})) %all-reduce.12.cloned.1.call-update) | async-done | bytes 811024 | tf_op jit(solution)/shard_map/psum | solution.py:272
  490.3 3.8 fusion.18
  495.6 53.2 %all-reduce.10.cloned.1.call-done = f32[32,512]{1,0:T(8,128)} async-done(((f32[32,512]{1,0:T(8,128)}), f32[32,512]{1,0:T(8,128)}) %all-reduce.10.cloned.1.call-update) | async-done | bytes 65552
  550.6 3.6 all-to-all-start.1
  554.3 6.3 gather_fusion.9
  560.6 6.1 broadcast_select_fusion.2
  566.7 4.6 all-to-all-start.3
  573.1 95.0 %all-to-all-done.3 = bf16[8,3,176,512]{3,2,1,0:T(8,128)(2,1)} async-done(((bf16[8,3,176,512]{3,2,1,0:T(8,128)(2,1)}), bf16[8,3,176,512]{3,2,1,0:T(8,128)(2,1)}, u32[]{:S(2)}, u32[]{:S(2)}) %all-to-all-start.3) | async-done | bytes 4325408 | tf_op jit(solution)/shard_map/all_to_all | solution.py:100
  668.1 2.5 copy.168
  670.9 11.0 %broadcast_select_fusion = bf16[4,2,1408,512]{3,2,1,0:T(8,128)(2,1)} fusion(bf16[4,2,1408,512]{3,2,1,0:T(8,128)(2,1)} %param.34, pred[4]{0:T(512)(128)(4,1)S(1)} %iota_compare_fusion.9, bf16[2,1408,512]{2,1,0:T(8,128)(2,1)S(1)} %slice_bitcast_fusion), kind=kLoop, calls=%fused_computation.21 | loop fusion | flops 5767168 | bytes 25952260 | tf_op jit(solution)/shard_map/jit(_where)/select_n | solution.py:102
  681.9 3.2 broadcast_select_fusion.1
  (205 shorter events, 53.8 us)
Async XLA Ops:
  7.2 541.6 %copy-start = (bf16[2816,512]{1,0:T(8,128)(2,1)S(1)}, bf16[2816,512]{1,0:T(8,128)(2,1)}, u32[]{:S(2)}) copy-start(bf16[2816,512]{1,0:T(8,128)(2,1)} %param.37) | copy-start | bytes 8650756
  9.3 2.3 copy-start.26
  10.8 1.6 copy-start.19
  71.3 6.5 copy-start.10
  71.3 210.8 %copy-start.16 = (f32[2048]{0:T(1024)S(1)}, f32[2048]{0:T(1024)}, u32[]{:S(2)}) copy-start(f32[2048]{0:T(1024)} %param.21) | copy-start | bytes 24580
  71.3 213.0 %copy-start.17 = (s32[32,16]{0,1:T(8,128)S(1)}, s32[32,16]{0,1:T(8,128)}, u32[]{:S(2)}) copy-start(s32[32,16]{0,1:T(8,128)} %param.27) | copy-start | bytes 6148
  71.3 479.3 %all-to-all-start.2 = ((bf16[2,3,8,176,512]{4,3,1,0,2:T(8,128)(2,1)}), bf16[2,3,8,176,512]{4,3,1,0,2:T(8,128)(2,1)}, u32[]{:S(2)}, u32[]{:S(2)}) async-start(bf16[2,3,8,176,512]{4,3,1,0,2:T(8,128)(2,1)} %copy.166), calls=%async_computation.2 | async-start | bytes 17301504 | tf_op jit(solution)/shard_map/all_to_all | solution.py:52
  77.7 327.9 %all-reduce.8.cloned.1.call-start = ((), (), s32[]{:S(2)}) async-start(), calls=%async_computation.4 | async-start | bytes 131072
  284.3 0.6 copy-start.3
  286.8 55.8 %copy-start.1 = (bf16[512,512]{0,1:T(8,128)(2,1)}, bf16[512,512]{0,1:T(8,128)(2,1)S(1)}, u32[]{:S(2)}) copy-start(bf16[512,512]{0,1:T(8,128)(2,1)S(1)} %copy.145) | copy-start | bytes 1572868
  287.8 0.6 copy-start.4
  291.7 2.0 copy-start.23
  292.3 0.6 copy-start.15
  293.6 0.6 copy-start.25
  295.1 0.6 copy-start.7
  295.1 0.6 copy-start.8
  302.9 3.3 copy-start.6
  331.3 0.8 copy-start.2
  332.9 12.5 %copy-start.13 = (f32[8,2]{0,1:T(2,128)}, f32[8,2]{0,1:T(2,128)S(1)}, u32[]{:S(2)}) copy-start(f32[8,2]{0,1:T(2,128)S(1)} %get-tuple-element.98) | copy-start | bytes 196
  333.8 11.6 %copy-start.9 = (f32[4,8,2,1]{1,0,3,2:T(4,128)}, f32[4,8,2,1]{1,0,3,2:T(4,128)S(1)}, u32[]{:S(2)}) copy-start(f32[4,8,2,1]{1,0,3,2:T(4,128)S(1)} %copy.182) | copy-start | bytes 772
  337.6 0.6 copy-start.5
  338.2 10.3 %copy-start.14 = (f32[4,8,2,1]{1,0,3,2:T(4,128)S(1)}, f32[4,8,2,1]{1,0,3,2:T(4,128)}, u32[]{:S(2)}) copy-start(f32[4,8,2,1]{1,0,3,2:T(4,128)} %copy.183) | copy-start | bytes 772
  338.2 14.2 %copy-start.21 = (s32[32,6]{0,1:T(8,128)S(1)}, s32[32,6]{0,1:T(8,128)}, u32[]{:S(2)}) copy-start(s32[32,6]{0,1:T(8,128)} %param.30) | copy-start | bytes 2308
  338.2 14.5 %copy-start.20 = (s32[32]{0:T(128)S(1)}, s32[32]{0:T(128)}, u32[]{:S(2)}) copy-start(s32[32]{0:T(128)} %copy-done.19) | copy-start | bytes 388
  338.2 33.5 %copy-start.22 = (f32[32,6]{0,1:T(8,128)S(1)}, f32[32,6]{0,1:T(8,128)}, u32[]{:S(2)}) copy-start(f32[32,6]{0,1:T(8,128)} %param.31) | copy-start | bytes 2308
  338.2 33.8 %copy-start.28 = (u32[32]{0:T(128)S(1)}, u32[32]{0:T(128)}, u32[]{:S(2)}) copy-start(u32[32]{0:T(128)} %constant.206) | copy-start | bytes 388
  338.3 67.3 %copy-start.11 = (bf16[1,2048]{1,0:T(2,128)(2,1)S(1)}, bf16[1,2048]{1,0:T(2,128)(2,1)}, u32[]{:S(2)}) copy-start(bf16[1,2048]{1,0:T(2,128)(2,1)} %param.20) | copy-start | bytes 12292
  338.3 70.1 %copy-start.18 = (f32[2048]{0:T(1024)S(1)}, f32[2048]{0:T(1024)}, u32[]{:S(2)}) copy-start(f32[2048]{0:T(1024)} %param.29) | copy-start | bytes 24580
  352.4 137.9 %all-reduce.12.cloned.1.call-start = ((), (), s32[]{:S(2)}) async-start(), calls=%async_computation.6 | async-start | bytes 1622016 | tf_op jit(solution)/shard_map/psum | solution.py:272
  442.7 106.1 %all-reduce.10.cloned.1.call-start = ((), (), s32[]{:S(2)}) async-start(), calls=%async_computation.5 | async-start | bytes 131072
  490.3 4.7 copy-start.24
  490.3 58.5 %copy-start.12 = (f32[2,4,2816]{2,1,0:T(4,128)S(1)}, f32[2,4,2816]{2,1,0:T(4,128)}, u32[]{:S(2)}) copy-start(f32[2,4,2816]{2,1,0:T(4,128)} %get-tuple-element.87) | copy-start | bytes 270340
  550.6 16.1 %all-to-all-start.1 = ((f32[4,1,512]{2,1,0:T(1,128)}), f32[4,1,512]{2,1,0:T(1,128)S(1)}, u32[]{:S(2)}, u32[]{:S(2)}) async-start(f32[4,1,512]{2,1,0:T(1,128)} %copy.164), calls=%async_computation.1 | async-start | bytes 16384 | tf_op jit(solution)/shard_map/all_to_all | solution.py:281
  566.7 4.6 copy-start.27
  566.7 101.4 %all-to-all-start.3 = ((bf16[8,3,176,512]{3,2,1,0:T(8,128)(2,1)}), bf16[8,3,176,512]{3,2,1,0:T(8,128)(2,1)}, u32[]{:S(2)}, u32[]{:S(2)}) async-start(bf16[8,3,176,512]{3,2,1,0:T(8,128)(2,1)} %broadcast_select_fusion.2), calls=%async_computation.3 | async-start | bytes 8650752 | tf_op jit(solution)/shard_map/all_to_all | solution.py:100
  670.6 11.3 %slice-start = ((s8[5767168]{0:T(1024)(128)(4,1)}), s8[4194304]{0:T(1024)(128)(4,1)S(1)}, s32[]{:S(2)}) async-start(s8[5767168]{0:T(1024)(128)(4,1)} %bitcast.223), calls=%async_computation.7 | async-start | bytes 8388608
  670.9 11.0 %slice-start.1 = ((s8[5767168]{0:T(1024)(128)(4,1)}), s8[1572864]{0:T(1024)(128)(4,1)S(1)}, s32[]{:S(2)}) async-start(s8[5767168]{0:T(1024)(128)(4,1)} %bitcast.223), calls=%async_computation.8 | async-start | bytes 3145728
Sparse Core Ops, SparseCore 0:
  352.5 53.0 all-reduce.7
  442.8 47.3 all-reduce.11
  495.1 53.6 all-reduce.9
where the time goes:
time: 694 us; the launch traced here: 692 us
  blocking collectives  238 us (34%)
  waiting for transfers between devices  228 us (33%)
  local copies, waits for them, and re-layouts  79.7 us (11%)
  other arithmetic  79.7 us (11%)
  matrix products  33.6 us (5%)
  between operations  18.1 us (3%)
  starting transfers between devices  14.8 us (2%)
    all_gather x2, blocking collectives, gather_rows(): by_expert = lax.all_gather(rows, 'expert', axis=0, tiled=True)  210 us
    all_to_all x1, waiting for transfers between devices, migrate(): lax.all_to_all(out_a, 'expert', split_axis=0, concat_axis=2, tiled=True)  95 us
    unnamed x5, waiting for transfers between devices  86.2 us
    psum x1, waiting for transfers between devices, local(): routed_sum, shared_sum = lax.psum((routed_part, shared_part), 'dp')  46.9 us
    gather x5, local copies, waits for them, and re-layouts, spread_slots(): chosen = jnp.concatenate([gate_up[picks], down[picks][:, None]], axis=1)  25.9 us
    all_gather x2, blocking collectives, gather_rows(): return lax.all_gather(by_expert, 'dp', axis=0, tiled=True)  16.9 us
  transfers between devices with their start and end apart: 6, of which 4 were waited for; matrix products, arithmetic and copies ran while one was open for 16% of the time, Pallas kernels for 0%

commit v1 on v0

--- a/solution.py
+++ b/solution.py
@@ -14,6 +14,12 @@
 ROPE_BASE = 50000.0
 MASKED_SCORE = -1e30
 HIGHEST = lax.Precision.HIGHEST
+
+
+def in_order(pieces, dim):
+    pieces = jnp.moveaxis(pieces, 0, dim)
+    dims = pieces.shape
+    return pieces.reshape(*dims[:dim], dims[dim] * dims[dim + 1], *dims[dim + 2 :])
 
 
 def rms_plain(values):
@@ -41,7 +47,19 @@
 
 
 def gather_rows(rows):
-    by_expert = lax.all_gather(rows, "expert", axis=0, tiled=True)
+    size = lax.axis_size("expert")
+    pairs = [(i, (i + 1) % size) for i in range(size)]
+    back = [(b, a) for a, b in pairs]
+    lower, upper = ([], [])
+    for step in range(size - 1):
+        if step % 2 == 0:
+            lower.append(lax.ppermute(lower[-1] if lower else rows, "expert", pairs))
+        else:
+            upper.append(lax.ppermute(upper[-1] if upper else rows, "expert", back))
+    blocks = jnp.stack([*lower[::-1], rows, *upper])
+    shift = lax.axis_index("expert") - len(lower)
+    blocks = blocks[(jnp.arange(size) - shift) % size]
+    by_expert = in_order(blocks, 0)
     return lax.all_gather(by_expert, "dp", axis=0, tiled=True)
 
 

time: 694 us -> 673 us (0.970)
  blocking collectives: 238 us -> 28.5 us
  waiting for transfers between devices: 228 us -> 377 us
  starting transfers between devices: 14.8 us -> 72.6 us
  local copies, waits for them, and re-layouts: 79.7 us -> 69.4 us
    all_gather x2 -> x0, blocking collectives: 210 us -> none  [gather_rows(): by_expert = lax.all_gather(rows, 'expert', axis=0, tiled=True)]
    ppermute x0 -> x14, waiting for transfers between devices: none -> 127 us  [the longest x8 124 us: gather_rows(): lower.append(lax.ppermute(lower[-1] if lower else rows, 'expert', pairs))]
    ppermute x0 -> x14, starting transfers between devices: none -> 57.8 us  [the longest x8 36.9 us: gather_rows(): lower.append(lax.ppermute(lower[-1] if lower else rows, 'expert', pairs))]
    unnamed x5, waiting for transfers between devices: 86.2 us -> 109 us
  transfers between devices with their start and end apart: 6 -> 20, of which waited for: 4 -> 11; matrix products, arithmetic and copies ran while one was open for 16% -> 14% of each run, Pallas kernels for 0% -> 0%
where the time goes in v1:
time: 673 us; the launch traced here: 671 us
  waiting for transfers between devices  377 us (56%)
  other arithmetic  73.8 us (11%)
  starting transfers between devices  72.6 us (11%)
  local copies, waits for them, and re-layouts  69.4 us (10%)
  matrix products  31.1 us (5%)
  blocking collectives  28.5 us (4%)
  between operations  18.4 us (3%)
    ppermute x8, waiting for transfers between devices, gather_rows(): lower.append(lax.ppermute(lower[-1] if lower else rows, 'expert', pairs))  124 us
    unnamed x5, waiting for transfers between devices  109 us
    all_to_all x1, waiting for transfers between devices, migrate(): lax.all_to_all(out_a, 'expert', split_axis=0, concat_axis=2, tiled=True)  95 us
    psum x1, waiting for transfers between devices, local(): routed_sum, shared_sum = lax.psum((routed_part, shared_part), 'dp')  46.1 us
    ppermute x8, starting transfers between devices, gather_rows(): lower.append(lax.ppermute(lower[-1] if lower else rows, 'expert', pairs))  36.9 us
    gather x5, local copies, waits for them, and re-layouts, spread_slots(): chosen = jnp.concatenate([gate_up[picks], down[picks][:, None]], axis=1)  25.9 us
    ppermute x6, starting transfers between devices, gather_rows(): upper.append(lax.ppermute(upper[-1] if upper else rows, 'expert', back))  20.8 us
    all_gather x2, blocking collectives, gather_rows(): return lax.all_gather(by_expert, 'dp', axis=0, tiled=True)  16.9 us
  transfers between devices with their start and end apart: 20, of which 11 were waited for; matrix products, arithmetic and copies ran while one was open for 14% of the time, Pallas kernels for 0%

profile of v1, /device:TPU:0, one launch (start us, length us, event | category | flops | bytes accessed | tf_op | source)
XLA Modules:
  0.0 670.7 jit_solution(3587788961913285687)
XLA Ops:
  18.3 5.9 mini-gather-slice.2
  24.2 5.2 mini-gather-slice.3
  30.9 5.2 gather_fusion.13
  36.1 4.7 gather_fusion.14
  40.8 5.0 gather_fusion.10
  45.8 5.6 pad_maximum_fusion.3
  51.4 7.7 %pad_maximum_fusion.2 = bf16[2,3,8,176,512]{4,3,2,1,0:T(8,128)(2,1)} fusion(bf16[2,1,8,176,512]{4,3,2,1,0:T(8,128)(2,1)} %bitcast.240, bf16[2,2,8,176,512]{4,3,2,1,0:T(8,128)(2,1)} %bitcast.236), kind=kLoop, calls=%fused_computation.24 | loop fusion | flops 4325376 | bytes 17301504 | tf_op jit(solution)/shard_map/concatenate | solution.py:67
  59.1 7.6 %copy.166 = bf16[2,3,8,176,512]{4,3,1,0,2:T(8,128)(2,1)} copy(bf16[2,3,8,176,512]{4,3,2,1,0:T(8,128)(2,1)} %pad_maximum_fusion.2) | data formatting | bytes 17301504 | tf_op jit(solution)/shard_map/concatenate | solution.py:67
  69.0 2.5 conditional.1
  69.0 2.5 broadcast.383
  71.6 6.5 all-to-all-start.2
  78.6 3.1 collective-permute-start.4
  82.3 2.4 scatter_custom_fusion
  87.3 4.3 compare_select_fusion.5
  92.3 11.1 %select_subtract_fusion = s32[192]{0:T(256)} fusion(pred[192]{0:T(512)(128)(4,1)S(1)} %get-tuple-element.86, pred[192]{0:T(512)(128)(4,1)S(1)} %get-tuple-element.85, pred[192]{0:T(512)(128)(4,1)S(1)} %get-tuple-element.84, pred[192]{0:T(512)(128)(4,1)S(1)} %get-tuple-element.83, pred[192]{0:T(512)(128)(4,1)S(1)} %get-tuple-element.82, ...), kind=kLoop, calls=%fused_computation.217 | loop fusion | flops 3456 | bytes 4872 | tf_op jit(solution)/shard_map/sub | solution.py:271
  104.2 117.7 %collective-permute-done = bf16[1,2048]{1,0:T(2,128)(2,1)S(1)} collective-permute-done((bf16[1,2048]{1,0:T(2,128)(2,1)S(1)}, bf16[1,2048]{1,0:T(2,128)(2,1)S(1)}, u32[]{:S(2)}, u32[]{:S(2)}) %collective-permute-start) | collective-permute-done | bytes 4128 | tf_op jit(solution)/shard_map/ppermute | solution.py:56
  222.0 3.6 collective-permute-start.5
  227.0 3.6 collective-permute-start.6
  231.9 36.4 %collective-permute-start.3 = (bf16[1,2048]{1,0:T(2,128)(2,1)S(1)}, bf16[1,2048]{1,0:T(2,128)(2,1)S(1)}, u32[]{:S(2)}, u32[]{:S(2)}) collective-permute-start(bf16[1,2048]{1,0:T(2,128)(2,1)S(1)} %collective-permute-done.2), channel_id=1, source_target_pairs={{0,1},{1,2},{2,3},{3,4},{4,5},{5,6},{6,7},{7,0},{8,9},{9,10},{10,1... | collective-permute-start | bytes 12296 | tf_op jit(solution)/shard_map/ppermute | solution.py:56
  271.6 8.5 %all-gather = bf16[32,2048]{1,0:T(8,128)(2,1)S(1)} all-gather(bf16[8,2048]{1,0:T(8,128)(2,1)S(1)} %gather_fusion.4), channel_id=2, replica_groups=mesh['dp'=4,'expert'=8] {'dp'}, dimensions={0}, use_global_device_ids=true | all-gather | bytes 163840 | tf_op jit(solution)/shard_map/all_gather | solution.py:63
  281.0 2.0 fusion.93
  285.7 1.7 gather_fusion.5
  287.4 1.6 fusion.6
  297.0 11.6 %all-gather.1 = f32[128,2,514]{2,0,1:T(8,128)S(1)} all-gather(f32[32,2,514]{2,0,1:T(8,128)S(1)} %pad_maximum_fusion.4), channel_id=3, replica_groups=mesh['dp'=4,'expert'=8] {'dp'}, dimensions={0}, use_global_device_ids=true | all-gather | bytes 657920 | tf_op jit(solution)/shard_map/all_gather | solution.py:208
  309.8 2.4 fusion.26
  315.5 1.7 copy.179
  317.2 3.0 multiply_reduce_fusion
  320.5 2.4 fusion.8
  323.5 55.4 %all-reduce.8.cloned.1.call-done = f32[8,2048]{1,0:T(8,128)} async-done(((f32[8,2048]{1,0:T(8,128)}), f32[8,2048]{1,0:T(8,128)}) %all-reduce.8.cloned.1.call-update) | async-done | bytes 65552
  378.9 2.1 multiply_reduce_fusion.2
  383.4 3.5 collective-permute-start.11
  388.3 3.5 collective-permute-start.12
  393.1 3.5 collective-permute-start.13
  398.0 3.5 collective-permute-done.10
  402.3 8.4 %all-gather.2 = bf16[32,2048]{1,0:T(8,128)(2,1)S(1)} all-gather(bf16[8,2048]{1,0:T(8,128)(2,1)S(1)} %gather_fusion.8), channel_id=4, replica_groups=mesh['dp'=4,'expert'=8] {'dp'}, dimensions={0}, use_global_device_ids=true | all-gather | bytes 163840 | tf_op jit(solution)/shard_map/all_gather | solution.py:63
  410.8 4.9 convolution_bitcast_fusion
  415.7 6.9 %convolution_bitcast_fusion.1 = f32[4,2,16,1408]{3,2,1,0:T(8,128)} fusion(bf16[4,2,1408,512]{3,2,1,0:T(8,128)(2,1)} %param.34, bf16[32,512,1]{1,0,2:T(8,128)(2,1)S(1)} %reshape.721, bf16[32,4,16]{0,2,1:T(8,128)(2,1)S(1)} %get-tuple-element.68), kind=kOutput, calls=%fused_computation.30 | convolution fusion | flops 186679296 | bytes 12292096 | tf_op jit(solution)/shard_map/scd,sgfd->sgcf/dot_general | solution.py:284
  423.3 46.1 %all-reduce.12.cloned.1.call-done = (f32[2,4,2816]{2,1,0:T(4,128)}, f32[4,2,16,1408]{3,2,1,0:T(8,128)}) async-done(((f32[2,4,2816]{2,1,0:T(4,128)}, f32[4,2,16,1408]{3,2,1,0:T(8,128)}), (f32[2,4,2816]{2,1,0:T(4,128)}, f32[4,2,16,1408]{3,2,1,0:T(8,128)})) %all-reduce.12.cloned.1.call-update) | async-done | bytes 811024 | tf_op jit(solution)/shard_map/psum | solution.py:290
  469.4 3.8 fusion.18
  474.7 53.1 %all-reduce.10.cloned.1.call-done = f32[32,512]{1,0:T(8,128)} async-done(((f32[32,512]{1,0:T(8,128)}), f32[32,512]{1,0:T(8,128)}) %all-reduce.10.cloned.1.call-update) | async-done | bytes 65552
  529.7 3.6 all-to-all-start.1
  533.3 6.3 gather_fusion.11
  539.7 6.1 broadcast_select_fusion.2
  545.8 4.6 all-to-all-start.3
  552.2 95.0 %all-to-all-done.3 = bf16[8,3,176,512]{3,2,1,0:T(8,128)(2,1)} async-done(((bf16[8,3,176,512]{3,2,1,0:T(8,128)(2,1)}), bf16[8,3,176,512]{3,2,1,0:T(8,128)(2,1)}, u32[]{:S(2)}, u32[]{:S(2)}) %all-to-all-start.3) | async-done | bytes 4325408 | tf_op jit(solution)/shard_map/all_to_all | solution.py:118
  647.1 2.5 copy.168
  650.0 11.0 %broadcast_select_fusion = bf16[4,2,1408,512]{3,2,1,0:T(8,128)(2,1)} fusion(bf16[4,2,1408,512]{3,2,1,0:T(8,128)(2,1)} %param.34, pred[4]{0:T(512)(128)(4,1)S(1)} %iota_compare_fusion.9, bf16[2,1408,512]{2,1,0:T(8,128)(2,1)S(1)} %slice_bitcast_fusion), kind=kLoop, calls=%fused_computation.23 | loop fusion | flops 5767168 | bytes 25952260 | tf_op jit(solution)/shard_map/jit(_where)/select_n | solution.py:120
  661.0 3.2 broadcast_select_fusion.1
  (223 shorter events, 52.5 us)
Async XLA Ops:
  7.2 520.7 %copy-start = (bf16[2816,512]{1,0:T(8,128)(2,1)S(1)}, bf16[2816,512]{1,0:T(8,128)(2,1)}, u32[]{:S(2)}) copy-start(bf16[2816,512]{1,0:T(8,128)(2,1)} %param.37) | copy-start | bytes 8650756
  9.3 2.3 copy-start.19
  71.6 6.5 copy-start.5
  71.6 10.2 %copy-start.15 = (s32[32,6]{0,1:T(8,128)S(1)}, s32[32,6]{0,1:T(8,128)}, u32[]{:S(2)}) copy-start(s32[32,6]{0,1:T(8,128)} %param.30) | copy-start | bytes 2308
  71.6 10.5 %copy-start.11 = (s32[32,16]{0,1:T(8,128)S(1)}, s32[32,16]{0,1:T(8,128)}, u32[]{:S(2)}) copy-start(s32[32,16]{0,1:T(8,128)} %param.27) | copy-start | bytes 6148
  71.6 20.1 %copy-start.21 = (s32[32]{0:T(128)S(1)}, s32[32]{0:T(128)}, u32[]{:S(2)}) copy-start(s32[32]{0:T(128)} %param.28) | copy-start | bytes 388
  71.6 208.7 %copy-start.12 = (f32[2048]{0:T(1024)S(1)}, f32[2048]{0:T(1024)}, u32[]{:S(2)}) copy-start(f32[2048]{0:T(1024)} %param.21) | copy-start | bytes 24580
  71.6 458.1 %all-to-all-start.2 = ((bf16[2,3,8,176,512]{4,3,1,0,2:T(8,128)(2,1)}), bf16[2,3,8,176,512]{4,3,1,0,2:T(8,128)(2,1)}, u32[]{:S(2)}, u32[]{:S(2)}) async-start(bf16[2,3,8,176,512]{4,3,1,0,2:T(8,128)(2,1)} %copy.166), calls=%async_computation.2 | async-start | bytes 17301504 | tf_op jit(solution)/shard_map/all_to_all | solution.py:70
  78.1 300.8 %all-reduce.8.cloned.1.call-start = ((), (), s32[]{:S(2)}) async-start(), calls=%async_computation.4 | async-start | bytes 131072
  78.1 143.8 %collective-permute-start = (bf16[1,2048]{1,0:T(2,128)(2,1)S(1)}, bf16[1,2048]{1,0:T(2,128)(2,1)S(1)}, u32[]{:S(2)}, u32[]{:S(2)}) collective-permute-start(bf16[1,2048]{1,0:T(2,128)(2,1)S(1)} %copy-done.5), channel_id=1, source_target_pairs={{0,1},{1,2},{2,3},{3,4},{4,5},{5,6},{6,7},{7,0},{8,9},{9,10},{10,1... | collective-permute-start | bytes 12296 | tf_op jit(solution)/shard_map/ppermute | solution.py:56
  78.6 143.3 %collective-permute-start.4 = (bf16[1,2048]{1,0:T(2,128)(2,1)S(1)}, bf16[1,2048]{1,0:T(2,128)(2,1)S(1)}, u32[]{:S(2)}, u32[]{:S(2)}) collective-permute-start(bf16[1,2048]{1,0:T(2,128)(2,1)S(1)} %copy-done.5), channel_id=1, source_target_pairs={{1,0},{2,1},{3,2},{4,3},{5,4},{6,5},{7,6},{0,7},{9,8},{10,9},{11,1... | collective-permute-start | bytes 12296 | tf_op jit(solution)/shard_map/ppermute | solution.py:58
  84.8 186.1 %copy-start.17 = (f32[32]{0:T(128)}, f32[32]{0:T(128)S(1)}, u32[]{:S(2)}) copy-start(f32[32]{0:T(128)S(1)} %multiply_exponential_fusion) | copy-start | bytes 388
  85.4 18.8 %copy-start.10 = (s32[32]{0:T(128)}, s32[32]{0:T(128)S(1)}, u32[]{:S(2)}) copy-start(s32[32]{0:T(128)S(1)} %get-tuple-element.101) | copy-start | bytes 388
  222.0 5.0 collective-permute-start.1
  222.0 5.0 collective-permute-start.5
  226.9 5.0 collective-permute-start.2
  226.9 53.3 %copy-start.14 = (s32[1024]{0:T(1024)}, s32[1024]{0:T(1024)S(1)}, u32[]{:S(2)}) copy-start(s32[1024]{0:T(1024)S(1)} %pad_clamp_fusion.6) | copy-start | bytes 12292
  227.0 43.9 %collective-permute-start.6 = (bf16[1,2048]{1,0:T(2,128)(2,1)S(1)}, bf16[1,2048]{1,0:T(2,128)(2,1)S(1)}, u32[]{:S(2)}, u32[]{:S(2)}) collective-permute-start(bf16[1,2048]{1,0:T(2,128)(2,1)S(1)} %collective-permute-done.5), channel_id=1, source_target_pairs={{1,0},{2,1},{3,2},{4,3},{5,4},{6,5},{7,6},{0,7},{9,8},{10,9},{11,1... | collective-permute-start | bytes 12296 | tf_op jit(solution)/shard_map/ppermute | solution.py:58
  231.9 38.9 %collective-permute-start.3 = (bf16[1,2048]{1,0:T(2,128)(2,1)S(1)}, bf16[1,2048]{1,0:T(2,128)(2,1)S(1)}, u32[]{:S(2)}, u32[]{:S(2)}) collective-permute-start(bf16[1,2048]{1,0:T(2,128)(2,1)S(1)} %collective-permute-done.2), channel_id=1, source_target_pairs={{0,1},{1,2},{2,3},{3,4},{4,5},{5,6},{6,7},{7,0},{8,9},{9,10},{10,1... | collective-permute-start | bytes 12296 | tf_op jit(solution)/shard_map/ppermute | solution.py:56
  270.1 38.5 %copy-start.1 = (bf16[512,512]{0,1:T(8,128)(2,1)}, bf16[512,512]{0,1:T(8,128)(2,1)S(1)}, u32[]{:S(2)}) copy-start(bf16[512,512]{0,1:T(8,128)(2,1)S(1)} %copy.145) | copy-start | bytes 1572868
  280.3 0.6 copy-start.3
  283.3 1.6 copy-start.4
  290.3 3.2 copy-start.7
  308.6 0.8 copy-start.2
  312.2 10.7 %copy-start.9 = (s32[192]{0:T(256)S(1)}, s32[192]{0:T(256)}, u32[]{:S(2)}) copy-start(s32[192]{0:T(256)} %select_subtract_fusion) | copy-start | bytes 2308
  312.2 10.8 %copy-start.22 = (u32[32]{0:T(128)S(1)}, u32[32]{0:T(128)}, u32[]{:S(2)}) copy-start(u32[32]{0:T(128)} %constant.224) | copy-start | bytes 388
  312.2 66.7 %copy-start.6 = (bf16[1,2048]{1,0:T(2,128)(2,1)S(1)}, bf16[1,2048]{1,0:T(2,128)(2,1)}, u32[]{:S(2)}) copy-start(bf16[1,2048]{1,0:T(2,128)(2,1)} %param.20) | copy-start | bytes 12292
  312.2 69.5 %copy-start.13 = (f32[2048]{0:T(1024)S(1)}, f32[2048]{0:T(1024)}, u32[]{:S(2)}) copy-start(f32[2048]{0:T(1024)} %param.29) | copy-start | bytes 24580
  312.2 79.8 %copy-start.16 = (f32[32,6]{0,1:T(8,128)S(1)}, f32[32,6]{0,1:T(8,128)}, u32[]{:S(2)}) copy-start(f32[32,6]{0,1:T(8,128)} %param.31) | copy-start | bytes 2308
  322.9 146.5 %all-reduce.12.cloned.1.call-start = ((), (), s32[]{:S(2)}) async-start(), calls=%async_computation.6 | async-start | bytes 1622016 | tf_op jit(solution)/shard_map/psum | solution.py:290
  381.7 5.2 collective-permute-start.7
  383.4 4.9 collective-permute-start.11
  386.9 4.9 collective-permute-start.8
  388.3 4.9 collective-permute-start.12
  391.8 4.9 collective-permute-start.9
  393.1 4.9 collective-permute-start.13
  396.7 4.9 collective-permute-start.10
  422.6 105.2 %all-reduce.10.cloned.1.call-start = ((), (), s32[]{:S(2)}) async-start(), calls=%async_computation.5 | async-start | bytes 131072
  469.4 4.7 copy-start.18
  469.4 58.5 %copy-start.8 = (f32[2,4,2816]{2,1,0:T(4,128)S(1)}, f32[2,4,2816]{2,1,0:T(4,128)}, u32[]{:S(2)}) copy-start(f32[2,4,2816]{2,1,0:T(4,128)} %get-tuple-element.87) | copy-start | bytes 270340
  529.7 16.1 %all-to-all-start.1 = ((f32[4,1,512]{2,1,0:T(1,128)}), f32[4,1,512]{2,1,0:T(1,128)S(1)}, u32[]{:S(2)}, u32[]{:S(2)}) async-start(f32[4,1,512]{2,1,0:T(1,128)} %copy.164), calls=%async_computation.1 | async-start | bytes 16384 | tf_op jit(solution)/shard_map/all_to_all | solution.py:299
  545.8 4.6 copy-start.20
  545.8 101.4 %all-to-all-start.3 = ((bf16[8,3,176,512]{3,2,1,0:T(8,128)(2,1)}), bf16[8,3,176,512]{3,2,1,0:T(8,128)(2,1)}, u32[]{:S(2)}, u32[]{:S(2)}) async-start(bf16[8,3,176,512]{3,2,1,0:T(8,128)(2,1)} %broadcast_select_fusion.2), calls=%async_computation.3 | async-start | bytes 8650752 | tf_op jit(solution)/shard_map/all_to_all | solution.py:118
  649.7 11.3 %slice-start = ((s8[5767168]{0:T(1024)(128)(4,1)}), s8[4194304]{0:T(1024)(128)(4,1)S(1)}, s32[]{:S(2)}) async-start(s8[5767168]{0:T(1024)(128)(4,1)} %bitcast.234), calls=%async_computation.7 | async-start | bytes 8388608
  650.0 11.0 %slice-start.1 = ((s8[5767168]{0:T(1024)(128)(4,1)}), s8[1572864]{0:T(1024)(128)(4,1)S(1)}, s32[]{:S(2)}) async-start(s8[5767168]{0:T(1024)(128)(4,1)} %bitcast.234), calls=%async_computation.8 | async-start | bytes 3145728
Sparse Core Ops, SparseCore 0:
  323.0 55.8 all-reduce.7
  422.7 46.5 all-reduce.11
  474.2 53.6 all-reduce.9
